TPU v7x, 512 devices: a whole 4x8x8 slice. The times are simulated.
512 devices in a mesh: ctx: 128 (over y, z, core), tp: 4 (over x).
Axes of the slice: x: 4, y: 8, z: 8, core: 2. Of those that a mesh axis runs over, the one named last changes fastest.
Arguments:
- hidden_in: bfloat16 [16384, 1536], P('ctx', 'tp'), may hold values from -60 to 60
- queries: bfloat16 [16384, 2048], P('ctx', 'tp'), may hold values from -200 to 200
- rotated_key_value: bfloat16 [16384, 4, 128], P('ctx', 'tp'), may hold values from -5 to 5
- sink_logit_table: float32 [32], P('tp'), may hold values from -2 to 2
- out_proj: bfloat16 [2048, 1536], P('tp', 'ctx'), may hold values from -0.125 to 0.125
- norm_gain: float32 [1536], P('tp'), may hold values from 0.1 to 1.9
- expert_in: bfloat16 [128, 2, 1536, 1536], P('ctx', None, None, 'tp'), may hold values from -0.15625 to 0.15625
- expert_out: bfloat16 [128, 1536, 1536], P('ctx', 'tp'), may hold values from -0.15625 to 0.15625
- routes: int32 [16384, 4], P('ctx'), may hold values from 0 to 127, all different within a row; in each aligned block of 128 rows (0 to 127, 128 to 255, ...) at most 12 rows name the same one
- route_scores: float32 [16384, 4], P('ctx'), may hold values from 0.05 to 1
Outputs:
- layer_out: bfloat16 [16384, 1536], P('ctx', 'tp')
Inputs may be any that keep to these rules, and one draw needn't show every extreme that they name: `routes`: each token names 4 different experts. In every aligned block of 128 tokens (the tokens of one device) no expert is named by more than 12 tokens, a bound that some block reaches.
All inputs are finite; a program needn't handle non-finite values.
Results may differ from a plain program's by a relative error of at most 0.008.
Values may be sent and summed in bfloat16 or wider, within the bound.
No kernel may reach another device: no remote copies, remote signals or barrier semaphores. Data moves between devices by JAX's collectives and lax.ppermute only.
A program may use at most 64 MiB of HBM per device.

v0:
```python
import jax
import jax.numpy as jnp
from jax import lax
from jax.sharding import PartitionSpec as P

WINDOW_KEYS = 128


def shifted(value, axis, steps):
    count = lax.axis_size(axis)
    first, last = (max(0, -steps), min(count, count - steps))
    return lax.ppermute(value, axis, [(source, source + steps) for source in range(first, last)])


def attend(query_block, key_blk, value_blk, inside, sink_row_block, factor):
    score = (
        jnp.einsum("rgqd,sgd->gqrs", query_block, key_blk, preferred_element_type=jnp.float32)
        * factor
    )
    masked = jnp.where(inside, score, -1e30)
    top_score = jnp.maximum(jnp.max(masked, -1), sink_row_block[:, :, None])
    expvals = jnp.where(inside, jnp.exp(score - top_score[..., None]), 0.0)
    denominator = jnp.sum(expvals, -1) + jnp.exp(sink_row_block[:, :, None] - top_score)
    probs = (expvals / denominator[..., None]).astype(jnp.bfloat16)
    mixed = jnp.einsum("gqrs,sgd->rgqd", probs, value_blk, preferred_element_type=jnp.float32)
    return mixed.astype(jnp.bfloat16)


def body(
    hidden_in,
    queries,
    rotated_key_value,
    sink_logit_table,
    out_proj,
    norm_gain,
    expert_in,
    expert_out,
    routes,
    route_scores,
):
    tok_rows = hidden_in.shape[0]
    kv_heads = rotated_key_value.shape[1]
    head_dim = rotated_key_value.shape[2] // 2
    q_heads = sink_logit_table.shape[0]
    queries_per_group = q_heads // kv_heads
    factor = head_dim ** (-0.5)
    sink_row_block = sink_logit_table.reshape(kv_heads, queries_per_group)
    earlier = shifted(rotated_key_value, "ctx", 1)
    keys_all = jnp.concatenate([earlier, rotated_key_value], 0)
    first_pos = lax.axis_index("ctx") * tok_rows
    block_row_count = min(512, tok_rows)
    query_block = queries.reshape(block_row_count, kv_heads, queries_per_group, head_dim)
    query_pos = first_pos + 0 + jnp.arange(block_row_count, dtype=jnp.int32)[:, None]
    key_pos = (
        first_pos
        + 0
        - WINDOW_KEYS
        + jnp.arange(block_row_count + WINDOW_KEYS, dtype=jnp.int32)[None, :]
    )
    inside = (key_pos <= query_pos) & (key_pos > query_pos - WINDOW_KEYS) & (key_pos >= 0)
    mixed = attend(
        query_block,
        keys_all[..., :head_dim],
        keys_all[..., head_dim:],
        inside,
        sink_row_block,
        factor,
    )
    outputs = mixed.reshape(block_row_count, q_heads * head_dim)
    head_partial = jnp.dot(
        outputs,
        lax.all_gather(out_proj, "ctx", axis=1, tiled=True),
        preferred_element_type=jnp.float32,
    )
    d_model = head_partial.shape[1]
    residual = hidden_in.astype(jnp.float32) + lax.psum_scatter(
        head_partial.astype(jnp.bfloat16), "tp", scatter_dimension=1, tiled=True
    ).astype(jnp.float32)
    square_total = lax.psum(jnp.sum(residual * residual, -1), "tp")
    normed = (residual * lax.rsqrt(square_total[:, None] / d_model + 1e-05) * norm_gain).astype(
        jnp.bfloat16
    )
    ctx_count = lax.axis_size("ctx")
    tp_count = lax.axis_size("tp")
    top_count = routes.shape[1]
    experts = ctx_count * expert_in.shape[0]
    capacity = max(2, min(tok_rows, 3 * top_count * tok_rows // experts))
    quarter_w = d_model // tp_count
    onehot = (routes[:, :, None] == jnp.arange(experts, dtype=jnp.int32)).astype(jnp.int32)
    per_tok = jnp.sum(onehot, 1)
    before = jnp.cumsum(per_tok, axis=0) - per_tok
    slot_ids = jnp.sum(onehot * before[:, None, :], -1)
    flat_index = (routes * capacity + slot_ids).reshape(-1)
    weights = route_scores / jnp.sum(route_scores, -1, keepdims=True)
    tp_index = lax.axis_index("tp")
    spread = jnp.broadcast_to(normed[:, None, :], (tok_rows, top_count, quarter_w)).reshape(
        -1, quarter_w
    )
    outbox = jnp.zeros((experts * capacity, quarter_w), jnp.bfloat16).at[flat_index].set(spread)
    arrived = lax.all_to_all(
        outbox.reshape(ctx_count, capacity, quarter_w), "ctx", 0, 0, tiled=True
    ).reshape(-1, quarter_w)
    pieces = [arrived]
    for step in range(1, tp_count):
        pieces.append(
            lax.ppermute(arrived, "tp", [(i, (i + step) % tp_count) for i in range(tp_count)])
        )
    row_data = jnp.concatenate(pieces, 1)
    order = (tp_index - jnp.arange(tp_count, dtype=jnp.int32)) % tp_count
    hidden_w = expert_in.shape[3]
    w_gate = jnp.take(
        expert_in[0, 0].reshape(tp_count, quarter_w, hidden_w), order, axis=0
    ).reshape(d_model, hidden_w)
    w_up = jnp.take(expert_in[0, 1].reshape(tp_count, quarter_w, hidden_w), order, axis=0).reshape(
        d_model, hidden_w
    )
    gate_vals = jnp.dot(row_data, w_gate, preferred_element_type=jnp.float32)
    up_vals = jnp.dot(row_data, w_up, preferred_element_type=jnp.float32)
    activated = ((up_vals + 1.0) * gate_vals * jax.nn.sigmoid(1.702 * gate_vals)).astype(
        jnp.bfloat16
    )

    def partial_for(quarter_id):
        cols = lax.dynamic_slice_in_dim(expert_out[0], quarter_id * quarter_w, quarter_w, 1)
        return jnp.dot(activated, cols, preferred_element_type=jnp.float32).astype(jnp.bfloat16)

    summed = partial_for(tp_index).astype(jnp.float32)
    for step in range(1, tp_count):
        piece = partial_for((tp_index + step) % tp_count)
        summed = summed + lax.ppermute(
            piece, "tp", [(i, (i + step) % tp_count) for i in range(tp_count)]
        ).astype(jnp.float32)
    result = summed.astype(jnp.bfloat16).reshape(ctx_count, capacity, quarter_w)
    returned = lax.all_to_all(result, "ctx", 0, 0, tiled=True).reshape(-1, quarter_w)
    expert_result = returned[flat_index].reshape(tok_rows, top_count, quarter_w)
    moe_sum = jnp.zeros((tok_rows, quarter_w), jnp.float32)
    for member in range(top_count):
        moe_sum = moe_sum + weights[:, member : member + 1] * expert_result[:, member].astype(
            jnp.float32
        )
    return (residual + moe_sum).astype(jnp.bfloat16)


def solution(mesh):
    in_specs = (
        P("ctx", "tp"),
        P("ctx", "tp"),
        P("ctx", "tp", None),
        P("tp"),
        P("tp", "ctx"),
        P("tp"),
        P("ctx", None, None, "tp"),
        P("ctx", "tp", None),
        P("ctx", None),
        P("ctx", None),
    )
    out_specs = P("ctx", "tp")
    return jax.shard_map(body, mesh=mesh, in_specs=in_specs, out_specs=out_specs, check_vma=False)
```

profile of v0, /device:TPU:8, one launch (start us, length us, event | category | flops | bytes accessed | tf_op | source)
XLA Modules:
  0.0 399.1 jit_solution(11350336013368773157)
XLA Ops:
  6.5 0.7 all-gather.3.cloned.1.call-update
  7.3 0.9 copy.35
  8.2 1.9 collective-permute-start
  10.3 1.0 copy.37
  11.3 8.7 %collective-permute-done = bf16[128,1,128]{0,2,1:T(8,128)(2,1)S(1)} collective-permute-done((bf16[128,1,128]{0,2,1:T(8,128)(2,1)S(1)}, bf16[128,1,128]{0,2,1:T(8,128)(2,1)S(1)}, u32[]{:S(2)}, u32[]{:S(2)}) %collective-permute-start) | collective-permute-done | bytes 32800 | tf_op jit(solution)/shard_map/ppermute | solution.py:12
  20.7 0.4 convolution_convert_fusion.5
  21.1 76.4 %all-gather.3.cloned.1.call-done = bf16[128,12,512]{2,1,0:T(8,128)(2,1)} async-done(((bf16[1,12,512]{2,1,0:T(8,128)(2,1)}), bf16[128,12,512]{2,1,0:T(8,128)(2,1)}) %all-gather.3.cloned.1.call-update) | async-done | bytes 1572880 | tf_op jit(solution)/shard_map/all_gather | solution.py:72
  97.5 2.5 reshape.245
  100.0 0.6 convolution_convert_fusion.4
  100.7 0.9 copy.44
  102.5 23.3 %reduce-scatter.4.cloned.1.call-done = bf16[384,128]{1,0:T(8,128)(2,1)} async-done(((bf16[1536,128]{1,0:T(8,128)(2,1)}), bf16[384,128]{1,0:T(8,128)(2,1)}) %reduce-scatter.4.cloned.1.call-update) | async-done | bytes 98320
  125.8 1.0 copy.45
  126.9 8.4 %psum.7 = f32[128]{0:T(128)S(1)} all-reduce(f32[128]{0:T(128)S(1)} %multiply_reduce_fusion), channel_id=1, replica_groups=mesh['ctx'=128,'tp'=4] {'tp'}, use_global_device_ids=true, to_apply=%region_8.9 | all-reduce | flops 128 | bytes 1024 | tf_op jit(solution)/shard_map/psum | solution.py:79
  135.7 3.5 scatter_custom_fusion
  139.2 2.2 reshape.199
  141.4 56.4 %all_to_all.10 = bf16[128,12,384]{2,1,0:T(8,128)(2,1)} all-to-all(bf16[128,12,384]{2,1,0:T(8,128)(2,1)S(1)} %reshape.199), channel_id=1, replica_groups=mesh['ctx'=128,'tp'=4] {'ctx'}, dimensions={0} | all-to-all | bytes 2359296 | tf_op jit(solution)/shard_map/all_to_all | solution.py:100
  197.8 3.2 reshape.200
  201.0 3.2 collective-permute-start.1
  204.2 2.9 fusion.38
  207.2 3.4 collective-permute-start.2
  210.6 3.3 collective-permute-start.3
  213.9 0.8 gather_fusion.1
  214.8 2.1 gather_fusion.2
  217.2 1.4 constant_dynamic-update-slice_fusion.3
  218.6 36.9 %collective-permute-done.1 = bf16[1536,384]{1,0:T(8,128)(2,1)} collective-permute-done((bf16[1536,384]{1,0:T(8,128)(2,1)}, bf16[1536,384]{1,0:T(8,128)(2,1)}, u32[]{:S(2)}, u32[]{:S(2)}) %collective-permute-start.1) | collective-permute-done | bytes 1179680 | tf_op jit(solution)/shard_map/ppermute | solution.py:106
  255.5 1.5 constant_dynamic-update-slice_fusion.2
  257.0 1.5 constant_dynamic-update-slice_fusion.1
  258.6 2.4 collective-permute-done.3
  261.0 1.5 constant_dynamic-update-slice_fusion
  262.5 2.6 fusion.40
  265.1 3.1 fusion.2
  268.2 1.9 convolution_convert_fusion.2
  270.1 2.9 collective-permute-start.4
  273.0 1.9 convolution_convert_fusion.1
  274.9 5.0 %collective-permute-start.5 = (bf16[1536,384]{1,0:T(8,128)(2,1)}, bf16[1536,384]{1,0:T(8,128)(2,1)}, u32[]{:S(2)}, u32[]{:S(2)}) collective-permute-start(bf16[1536,384]{1,0:T(8,128)(2,1)} %convolution_convert_fusion.1), channel_id=1, source_target_pairs={{0,2},{1,3},{2,0},{3,1},{4,6},{5,7},{6,4},{7,5},{8,10},{9,11},{10,... | collective-permute-start | bytes 3538952 | tf_op jit(solution)/shard_map/ppermute | solution.py:130
  279.9 1.9 convolution_convert_fusion
  281.8 2.1 collective-permute-start.6
  283.9 17.1 %collective-permute-done.4 = bf16[1536,384]{1,0:T(8,128)(2,1)S(1)} collective-permute-done((bf16[1536,384]{1,0:T(8,128)(2,1)}, bf16[1536,384]{1,0:T(8,128)(2,1)S(1)}, u32[]{:S(2)}, u32[]{:S(2)}) %collective-permute-start.4) | collective-permute-done | bytes 1179680 | tf_op jit(solution)/shard_map/ppermute | solution.py:130
  301.0 26.6 %collective-permute-done.5 = bf16[1536,384]{1,0:T(8,128)(2,1)} collective-permute-done((bf16[1536,384]{1,0:T(8,128)(2,1)}, bf16[1536,384]{1,0:T(8,128)(2,1)}, u32[]{:S(2)}, u32[]{:S(2)}) %collective-permute-start.5) | collective-permute-done | bytes 1179680 | tf_op jit(solution)/shard_map/ppermute | solution.py:130
  327.6 3.3 collective-permute-done.6
  330.8 3.1 add_convert_fusion
  333.9 1.3 reshape.203
  335.2 9.0 %all-to-all-start.1 = ((bf16[128,12,384]{2,1,0:T(8,128)(2,1)}), bf16[128,12,384]{2,1,0:T(8,128)(2,1)}, u32[]{:S(2)}, u32[]{:S(2)}) async-start(bf16[128,12,384]{2,1,0:T(8,128)(2,1)} %reshape.203), calls=%async_computation.1 | async-start | bytes 3145728 | tf_op jit(solution)/shard_map/all_to_all | solution.py:134
  344.3 42.0 %all-to-all-done.1 = bf16[128,12,384]{2,1,0:T(8,128)(2,1)} async-done(((bf16[128,12,384]{2,1,0:T(8,128)(2,1)}), bf16[128,12,384]{2,1,0:T(8,128)(2,1)}, u32[]{:S(2)}, u32[]{:S(2)}) %all-to-all-start.1) | async-done | bytes 1179680 | tf_op jit(solution)/shard_map/all_to_all | solution.py:134
  386.3 2.3 reshape.204
  388.6 1.9 gather_fusion
  390.6 0.6 fusion.39
  391.5 0.8 fusion.21
  (54 shorter events, 2.9 us)
Async XLA Ops:
  6.5 261.6 %copy-start = (bf16[1,384,1536]{2,1,0:T(8,128)(2,1)S(1)}, bf16[1,384,1536]{2,1,0:T(8,128)(2,1)}, u32[]{:S(2)}) copy-start(bf16[1,384,1536]{2,1,0:T(8,128)(2,1)} %param.19) | copy-start | bytes 3538948
  6.5 13.8 %copy-start.9 = (f32[8]{0:T(128)S(1)}, f32[8]{0:T(128)}, u32[]{:S(2)}) copy-start(f32[8]{0:T(128)} %param.15) | copy-start | bytes 100
  6.5 91.0 %all-gather.3.cloned.1.call-start = ((), (), s32[]{:S(2)}) async-start(), calls=%async_computation.3 | async-start | bytes 2113536 | tf_op jit(solution)/shard_map/all_gather | solution.py:72
  7.3 118.5 %reduce-scatter.4.cloned.1.call-start = ((), (), s32[]{:S(2)}) async-start(), calls=%async_computation.4 | async-start | bytes 491520
  8.2 11.9 %collective-permute-start = (bf16[128,1,128]{0,2,1:T(8,128)(2,1)S(1)}, bf16[128,1,128]{0,2,1:T(8,128)(2,1)S(1)}, u32[]{:S(2)}, u32[]{:S(2)}) collective-permute-start(bf16[128,1,128]{0,2,1:T(8,128)(2,1)S(1)} %copy.35), channel_id=1, source_target_pairs={{0,4},{4,8},{8,12},{12,16},{16,20},{20,24},{24,28},{28,32},{32,36}... | collective-permute-start | bytes 98312 | tf_op jit(solution)/shard_map/ppermute | solution.py:12
  100.0 1.6 copy-start.6
  100.6 26.2 %copy-start.4 = (bf16[128,384]{1,0:T(8,128)(2,1)S(1)}, bf16[128,384]{1,0:T(8,128)(2,1)}, u32[]{:S(2)}) copy-start(bf16[128,384]{1,0:T(8,128)(2,1)} %param.12) | copy-start | bytes 294916
  100.7 34.7 %copy-start.8 = (f32[384]{0:T(512)S(1)}, f32[384]{0:T(512)}, u32[]{:S(2)}) copy-start(f32[384]{0:T(512)} %param.17) | copy-start | bytes 4612
  126.8 8.9 %copy-start.1 = (bf16[128,384]{1,0:T(8,128)(2,1)}, bf16[128,384]{1,0:T(8,128)(2,1)S(1)}, u32[]{:S(2)}) copy-start(bf16[128,384]{1,0:T(8,128)(2,1)S(1)} %copy.45) | copy-start | bytes 294916
  201.0 54.5 %collective-permute-start.1 = (bf16[1536,384]{1,0:T(8,128)(2,1)}, bf16[1536,384]{1,0:T(8,128)(2,1)}, u32[]{:S(2)}, u32[]{:S(2)}) collective-permute-start(bf16[1536,384]{1,0:T(8,128)(2,1)} %reshape.200), channel_id=1, source_target_pairs={{0,1},{1,2},{2,3},{3,0},{4,5},{5,6},{6,7},{7,4},{8,9},{9,10},{10,1... | collective-permute-start | bytes 3538952 | tf_op jit(solution)/shard_map/ppermute | solution.py:106
  207.2 49.9 %collective-permute-start.2 = (bf16[1536,384]{1,0:T(8,128)(2,1)}, bf16[1536,384]{1,0:T(8,128)(2,1)}, u32[]{:S(2)}, u32[]{:S(2)}) collective-permute-start(bf16[1536,384]{1,0:T(8,128)(2,1)} %reshape.200), channel_id=1, source_target_pairs={{0,2},{1,3},{2,0},{3,1},{4,6},{5,7},{6,4},{7,5},{8,10},{9,11},{10,... | collective-permute-start | bytes 3538952 | tf_op jit(solution)/shard_map/ppermute | solution.py:106
  210.6 50.4 %collective-permute-start.3 = (bf16[1536,384]{1,0:T(8,128)(2,1)}, bf16[1536,384]{1,0:T(8,128)(2,1)}, u32[]{:S(2)}, u32[]{:S(2)}) collective-permute-start(bf16[1536,384]{1,0:T(8,128)(2,1)} %reshape.200), channel_id=1, source_target_pairs={{0,3},{1,0},{2,1},{3,2},{4,7},{5,4},{6,5},{7,6},{8,11},{9,8},{10,9... | collective-permute-start | bytes 3538952 | tf_op jit(solution)/shard_map/ppermute | solution.py:106
  270.1 30.9 %collective-permute-start.4 = (bf16[1536,384]{1,0:T(8,128)(2,1)}, bf16[1536,384]{1,0:T(8,128)(2,1)S(1)}, u32[]{:S(2)}, u32[]{:S(2)}) collective-permute-start(bf16[1536,384]{1,0:T(8,128)(2,1)} %convolution_convert_fusion.2), channel_id=1, source_target_pairs={{0,1},{1,2},{2,3},{3,0},{4,5},{5,6},{6,7},{7,4},{8,9},{9,10},{10,1... | collective-permute-start | bytes 3538952 | tf_op jit(solution)/shard_map/ppermute | solution.py:130
  274.9 52.6 %collective-permute-start.5 = (bf16[1536,384]{1,0:T(8,128)(2,1)}, bf16[1536,384]{1,0:T(8,128)(2,1)}, u32[]{:S(2)}, u32[]{:S(2)}) collective-permute-start(bf16[1536,384]{1,0:T(8,128)(2,1)} %convolution_convert_fusion.1), channel_id=1, source_target_pairs={{0,2},{1,3},{2,0},{3,1},{4,6},{5,7},{6,4},{7,5},{8,10},{9,11},{10,... | collective-permute-start | bytes 3538952 | tf_op jit(solution)/shard_map/ppermute | solution.py:130
  281.8 49.0 %collective-permute-start.6 = (bf16[1536,384]{1,0:T(8,128)(2,1)}, bf16[1536,384]{1,0:T(8,128)(2,1)}, u32[]{:S(2)}, u32[]{:S(2)}) collective-permute-start(bf16[1536,384]{1,0:T(8,128)(2,1)} %convolution_convert_fusion), channel_id=1, source_target_pairs={{0,3},{1,0},{2,1},{3,2},{4,7},{5,4},{6,5},{7,6},{8,11},{9,8},{10,9... | collective-permute-start | bytes 3538952 | tf_op jit(solution)/shard_map/ppermute | solution.py:130
  301.0 26.6 %copy-start.3 = (bf16[1536,384]{1,0:T(8,128)(2,1)}, bf16[1536,384]{1,0:T(8,128)(2,1)S(1)}, u32[]{:S(2)}) copy-start(bf16[1536,384]{1,0:T(8,128)(2,1)S(1)} %collective-permute-done.4) | copy-start | bytes 3538948
  335.2 9.1 %copy-start.7 = (f32[128,4]{0,1:T(4,128)S(1)}, f32[128,4]{0,1:T(4,128)}, u32[]{:S(2)}) copy-start(f32[128,4]{0,1:T(4,128)} %param.21) | copy-start | bytes 6148
  335.2 51.1 %all-to-all-start.1 = ((bf16[128,12,384]{2,1,0:T(8,128)(2,1)}), bf16[128,12,384]{2,1,0:T(8,128)(2,1)}, u32[]{:S(2)}, u32[]{:S(2)}) async-start(bf16[128,12,384]{2,1,0:T(8,128)(2,1)} %reshape.203), calls=%async_computation.1 | async-start | bytes 3145728 | tf_op jit(solution)/shard_map/all_to_all | solution.py:134
  390.5 0.9 copy-start.2
  390.5 0.9 copy-start.5
Sparse Core Ops, SparseCore 0:
  10.5 86.9 all-gather.2
  101.7 23.9 reduce-scatter.3
where the time goes:
time: 400 us; the launch traced here: 399 us
  waiting for transfers between devices  237 us (59%)
  blocking collectives  64.8 us (16%)
  local copies, waits for them, and re-layouts  33.3 us (8%)
  starting transfers between devices  30.9 us (8%)
  matrix products  15.8 us (4%)
  between operations  13.9 us (3%)
    all_gather x1, waiting for transfers between devices, body(): lax.all_gather(out_proj, 'ctx', axis=1, tiled=True)  76.4 us
    all_to_all x1, blocking collectives, body(): lax.all_to_all(outbox.reshape(ctx_count, capacity, quarter_w), 'ctx', 0,...  56.4 us
    ppermute x3, waiting for transfers between devices, body(): lax.ppermute(piece, 'tp', [(i, (i + step) % tp_count) for i in range(tp_c...  46.9 us
    all_to_all x1, waiting for transfers between devices, body(): lax.all_to_all(result, 'ctx', 0, 0, tiled=True).reshape(-1, quarter_w)  42 us
    ppermute x3, waiting for transfers between devices, body(): lax.ppermute(arrived, 'tp', [(i, (i + step) % tp_count) for i in range(tp...  39.3 us
    unnamed x3, waiting for transfers between devices  24.1 us
    unnamed x28, local copies, waits for them, and re-layouts  11 us
    ppermute x3, starting transfers between devices, body(): lax.ppermute(piece, 'tp', [(i, (i + step) % tp_count) for i in range(tp_c...  9.97 us
  transfers between devices with their start and end apart: 10, of which 9 were waited for; matrix products, arithmetic and copies ran while one was open for 5% of the time, Pallas kernels for 0%

commit v1 on v0

--- a/solution.py
+++ b/solution.py
@@ -4,6 +4,13 @@
 from jax.sharding import PartitionSpec as P
 
 WINDOW_KEYS = 128
+
+
+def all_by_exchange(block, axis, d):
+    n_dev = lax.axis_size(axis)
+    shards = jnp.stack([block for _ in range(n_dev)])
+    shards = lax.all_to_all(shards, axis, split_axis=0, concat_axis=0)
+    return jnp.concatenate(shards, axis=d)
 
 
 def shifted(value, axis, steps):
@@ -68,9 +75,7 @@
     )
     outputs = mixed.reshape(block_row_count, q_heads * head_dim)
     head_partial = jnp.dot(
-        outputs,
-        lax.all_gather(out_proj, "ctx", axis=1, tiled=True),
-        preferred_element_type=jnp.float32,
+        outputs, all_by_exchange(out_proj, "ctx", 1), preferred_element_type=jnp.float32
     )
     d_model = head_partial.shape[1]
     residual = hidden_in.astype(jnp.float32) + lax.psum_scatter(

time: 400 us -> 380 us (0.950)
  waiting for transfers between devices: 237 us -> 197 us
  starting transfers between devices: 30.9 us -> 48.4 us
    all_gather x1 -> x0, waiting for transfers between devices: 76.4 us -> none  [body(): lax.all_gather(out_proj, 'ctx', axis=1, tiled=True)]
    ppermute x1, waiting for transfers between devices: 8.72 us -> 42.7 us  [shifted(): lax.ppermute(value, axis, [(source, source + steps) for source in range(f...]
    all_to_all x0 -> x1, starting transfers between devices: none -> 17.5 us  [all_by_exchange(): shards = lax.all_to_all(shards, axis, split_axis=0, concat_axis=0)]
    all_to_all x0 -> x1, waiting for transfers between devices: none -> 5.22 us  [all_by_exchange(): shards = lax.all_to_all(shards, axis, split_axis=0, concat_axis=0)]
    unnamed x28 -> x29, local copies, waits for them, and re-layouts: 11 us -> 7.79 us
    unnamed x3 -> x2, waiting for transfers between devices: 24.1 us -> 21.3 us
where the time goes in v1:
time: 380 us; the launch traced here: 379 us
  waiting for transfers between devices  197 us (52%)
  blocking collectives  64.9 us (17%)
  starting transfers between devices  48.4 us (13%)
  local copies, waits for them, and re-layouts  33.8 us (9%)
  matrix products  17.3 us (5%)
  between operations  13.9 us (4%)
    all_to_all x1, blocking collectives, body(): lax.all_to_all(outbox.reshape(ctx_count, capacity, quarter_w), 'ctx', 0,...  56.4 us
    ppermute x3, waiting for transfers between devices, body(): lax.ppermute(piece, 'tp', [(i, (i + step) % tp_count) for i in range(tp_c...  46.9 us
    ppermute x1, waiting for transfers between devices, shifted(): lax.ppermute(value, axis, [(source, source + steps) for source in range(f...  42.7 us
    all_to_all x1, waiting for transfers between devices, body(): lax.all_to_all(result, 'ctx', 0, 0, tiled=True).reshape(-1, quarter_w)  42 us
    ppermute x3, waiting for transfers between devices, body(): lax.ppermute(arrived, 'tp', [(i, (i + step) % tp_count) for i in range(tp...  39.3 us
    unnamed x2, waiting for transfers between devices  21.3 us
    all_to_all x1, starting transfers between devices, all_by_exchange(): shards = lax.all_to_all(shards, axis, split_axis=0, concat_axis=0)  17.5 us
    ppermute x3, starting transfers between devices, body(): lax.ppermute(piece, 'tp', [(i, (i + step) % tp_count) for i in range(tp_c...  9.94 us
  transfers between devices with their start and end apart: 10, of which 9 were waited for; matrix products, arithmetic and copies ran while one was open for 5% of the time, Pallas kernels for 0%

profile of v1, /device:TPU:8, one launch (start us, length us, event | category | flops | bytes accessed | tf_op | source)
XLA Modules:
  0.0 378.7 jit_solution(17346620535380411034)
XLA Ops:
  6.5 2.4 stack.2
  9.0 17.5 %all-to-all-start = ((bf16[128,512,12]{1,2,0:T(8,128)(2,1)}), bf16[128,512,12]{1,2,0:T(8,128)(2,1)S(1)}, u32[]{:S(2)}, u32[]{:S(2)}) async-start(bf16[128,512,12]{1,2,0:T(8,128)(2,1)} %stack.2), calls=%async_computation | async-start | bytes 4194304 | tf_op jit(solution)/shard_map/all_to_all | solution.py:12
  26.6 2.0 collective-permute-start
  28.9 1.0 copy.38
  29.9 42.7 %collective-permute-done = bf16[128,1,128]{0,2,1:T(8,128)(2,1)S(1)} collective-permute-done((bf16[128,1,128]{0,2,1:T(8,128)(2,1)S(1)}, bf16[128,1,128]{0,2,1:T(8,128)(2,1)S(1)}, u32[]{:S(2)}, u32[]{:S(2)}) %collective-permute-start) | collective-permute-done | bytes 32800 | tf_op jit(solution)/shard_map/ppermute | solution.py:19
  73.3 0.4 convolution_convert_fusion.5
  73.6 5.2 %all-to-all-done = bf16[128,512,12]{1,2,0:T(8,128)(2,1)S(1)} async-done(((bf16[128,512,12]{1,2,0:T(8,128)(2,1)}), bf16[128,512,12]{1,2,0:T(8,128)(2,1)S(1)}, u32[]{:S(2)}, u32[]{:S(2)}) %all-to-all-start) | async-done | bytes 1572896 | tf_op jit(solution)/shard_map/all_to_all | solution.py:12
  78.8 1.3 reshape.206
  80.2 2.1 convolution_convert_fusion.4
  82.3 0.9 copy.45
  84.1 21.3 %reduce-scatter.4.cloned.1.call-done = bf16[384,128]{1,0:T(8,128)(2,1)} async-done(((bf16[1536,128]{1,0:T(8,128)(2,1)}), bf16[384,128]{1,0:T(8,128)(2,1)}) %reduce-scatter.4.cloned.1.call-update) | async-done | bytes 98320
  105.3 1.0 copy.46
  106.5 8.5 %psum.7 = f32[128]{0:T(128)S(1)} all-reduce(f32[128]{0:T(128)S(1)} %multiply_reduce_fusion), channel_id=1, replica_groups=mesh['ctx'=128,'tp'=4] {'tp'}, use_global_device_ids=true, to_apply=%region_8.9 | all-reduce | flops 128 | bytes 1024 | tf_op jit(solution)/shard_map/psum | solution.py:84
  115.3 3.5 scatter_custom_fusion
  118.8 2.2 reshape.209
  121.0 56.4 %all_to_all.15 = bf16[128,12,384]{2,1,0:T(8,128)(2,1)} all-to-all(bf16[128,12,384]{2,1,0:T(8,128)(2,1)S(1)} %reshape.209), channel_id=1, replica_groups=mesh['ctx'=128,'tp'=4] {'ctx'}, dimensions={0} | all-to-all | bytes 2359296 | tf_op jit(solution)/shard_map/all_to_all | solution.py:105
  177.4 3.2 reshape.210
  180.6 3.2 collective-permute-start.1
  183.8 2.9 fusion.38
  186.7 3.4 collective-permute-start.2
  190.1 3.3 collective-permute-start.3
  193.5 0.8 gather_fusion.1
  194.3 2.1 gather_fusion.2
  196.8 1.4 constant_dynamic-update-slice_fusion.3
  198.2 36.9 %collective-permute-done.1 = bf16[1536,384]{1,0:T(8,128)(2,1)} collective-permute-done((bf16[1536,384]{1,0:T(8,128)(2,1)}, bf16[1536,384]{1,0:T(8,128)(2,1)}, u32[]{:S(2)}, u32[]{:S(2)}) %collective-permute-start.1) | collective-permute-done | bytes 1179680 | tf_op jit(solution)/shard_map/ppermute | solution.py:111
  235.1 1.5 constant_dynamic-update-slice_fusion.2
  236.6 1.5 constant_dynamic-update-slice_fusion.1
  238.2 2.4 collective-permute-done.3
  240.6 1.5 constant_dynamic-update-slice_fusion
  242.1 2.6 fusion.40
  244.7 3.1 fusion.2
  247.8 1.9 convolution_convert_fusion.2
  249.7 2.9 collective-permute-start.4
  252.6 1.9 convolution_convert_fusion.1
  254.5 5.0 %collective-permute-start.5 = (bf16[1536,384]{1,0:T(8,128)(2,1)}, bf16[1536,384]{1,0:T(8,128)(2,1)}, u32[]{:S(2)}, u32[]{:S(2)}) collective-permute-start(bf16[1536,384]{1,0:T(8,128)(2,1)} %convolution_convert_fusion.1), channel_id=1, source_target_pairs={{0,2},{1,3},{2,0},{3,1},{4,6},{5,7},{6,4},{7,5},{8,10},{9,11},{10,... | collective-permute-start | bytes 3538952 | tf_op jit(solution)/shard_map/ppermute | solution.py:135
  259.5 1.9 convolution_convert_fusion
  261.4 2.1 collective-permute-start.6
  263.5 17.1 %collective-permute-done.4 = bf16[1536,384]{1,0:T(8,128)(2,1)S(1)} collective-permute-done((bf16[1536,384]{1,0:T(8,128)(2,1)}, bf16[1536,384]{1,0:T(8,128)(2,1)S(1)}, u32[]{:S(2)}, u32[]{:S(2)}) %collective-permute-start.4) | collective-permute-done | bytes 1179680 | tf_op jit(solution)/shard_map/ppermute | solution.py:135
  280.6 26.6 %collective-permute-done.5 = bf16[1536,384]{1,0:T(8,128)(2,1)} collective-permute-done((bf16[1536,384]{1,0:T(8,128)(2,1)}, bf16[1536,384]{1,0:T(8,128)(2,1)}, u32[]{:S(2)}, u32[]{:S(2)}) %collective-permute-start.5) | collective-permute-done | bytes 1179680 | tf_op jit(solution)/shard_map/ppermute | solution.py:135
  307.2 3.2 collective-permute-done.6
  310.4 3.1 add_convert_fusion
  313.5 1.3 reshape.213
  314.8 9.1 %all-to-all-start.2 = ((bf16[128,12,384]{2,1,0:T(8,128)(2,1)}), bf16[128,12,384]{2,1,0:T(8,128)(2,1)}, u32[]{:S(2)}, u32[]{:S(2)}) async-start(bf16[128,12,384]{2,1,0:T(8,128)(2,1)} %reshape.213), calls=%async_computation.2 | async-start | bytes 3145728 | tf_op jit(solution)/shard_map/all_to_all | solution.py:139
  323.9 42.0 %all-to-all-done.2 = bf16[128,12,384]{2,1,0:T(8,128)(2,1)} async-done(((bf16[128,12,384]{2,1,0:T(8,128)(2,1)}), bf16[128,12,384]{2,1,0:T(8,128)(2,1)}, u32[]{:S(2)}, u32[]{:S(2)}) %all-to-all-start.2) | async-done | bytes 1179680 | tf_op jit(solution)/shard_map/all_to_all | solution.py:139
  365.9 2.3 reshape.214
  368.2 1.9 gather_fusion
  370.2 0.6 fusion.39
  371.1 0.8 fusion.21
  (56 shorter events, 3.0 us)
Async XLA Ops:
  6.5 241.2 %copy-start = (bf16[1,384,1536]{2,1,0:T(8,128)(2,1)S(1)}, bf16[1,384,1536]{2,1,0:T(8,128)(2,1)}, u32[]{:S(2)}) copy-start(bf16[1,384,1536]{2,1,0:T(8,128)(2,1)} %param.19) | copy-start | bytes 3538948
  8.9 17.6 %copy-start.6 = (bf16[128,1,128]{2,0,1:T(8,128)(2,1)S(1)}, bf16[128,1,128]{2,0,1:T(8,128)(2,1)}, u32[]{:S(2)}) copy-start(bf16[128,1,128]{2,0,1:T(8,128)(2,1)} %param.14) | copy-start | bytes 98308
  9.0 69.9 %all-to-all-start = ((bf16[128,512,12]{1,2,0:T(8,128)(2,1)}), bf16[128,512,12]{1,2,0:T(8,128)(2,1)S(1)}, u32[]{:S(2)}, u32[]{:S(2)}) async-start(bf16[128,512,12]{1,2,0:T(8,128)(2,1)} %stack.2), calls=%async_computation | async-start | bytes 4194304 | tf_op jit(solution)/shard_map/all_to_all | solution.py:12
  26.5 46.4 %copy-start.10 = (f32[8]{0:T(128)S(1)}, f32[8]{0:T(128)}, u32[]{:S(2)}) copy-start(f32[8]{0:T(128)} %param.15) | copy-start | bytes 100
  26.5 78.9 %reduce-scatter.4.cloned.1.call-start = ((), (), s32[]{:S(2)}) async-start(), calls=%async_computation.4 | async-start | bytes 491520
  26.6 45.9 %collective-permute-start = (bf16[128,1,128]{0,2,1:T(8,128)(2,1)S(1)}, bf16[128,1,128]{0,2,1:T(8,128)(2,1)S(1)}, u32[]{:S(2)}, u32[]{:S(2)}) collective-permute-start(bf16[128,1,128]{0,2,1:T(8,128)(2,1)S(1)} %copy.36), channel_id=1, source_target_pairs={{0,4},{4,8},{8,12},{12,16},{16,20},{20,24},{24,28},{28,32},{32,36}... | collective-permute-start | bytes 98312 | tf_op jit(solution)/shard_map/ppermute | solution.py:19
  80.2 3.1 copy-start.7
  82.3 24.1 %copy-start.4 = (bf16[128,384]{1,0:T(8,128)(2,1)S(1)}, bf16[128,384]{1,0:T(8,128)(2,1)}, u32[]{:S(2)}) copy-start(bf16[128,384]{1,0:T(8,128)(2,1)} %param.12) | copy-start | bytes 294916
  82.3 32.7 %copy-start.9 = (f32[384]{0:T(512)S(1)}, f32[384]{0:T(512)}, u32[]{:S(2)}) copy-start(f32[384]{0:T(512)} %param.17) | copy-start | bytes 4612
  106.4 8.9 %copy-start.1 = (bf16[128,384]{1,0:T(8,128)(2,1)}, bf16[128,384]{1,0:T(8,128)(2,1)S(1)}, u32[]{:S(2)}) copy-start(bf16[128,384]{1,0:T(8,128)(2,1)S(1)} %copy.46) | copy-start | bytes 294916
  180.6 54.5 %collective-permute-start.1 = (bf16[1536,384]{1,0:T(8,128)(2,1)}, bf16[1536,384]{1,0:T(8,128)(2,1)}, u32[]{:S(2)}, u32[]{:S(2)}) collective-permute-start(bf16[1536,384]{1,0:T(8,128)(2,1)} %reshape.210), channel_id=1, source_target_pairs={{0,1},{1,2},{2,3},{3,0},{4,5},{5,6},{6,7},{7,4},{8,9},{9,10},{10,1... | collective-permute-start | bytes 3538952 | tf_op jit(solution)/shard_map/ppermute | solution.py:111
  186.7 49.9 %collective-permute-start.2 = (bf16[1536,384]{1,0:T(8,128)(2,1)}, bf16[1536,384]{1,0:T(8,128)(2,1)}, u32[]{:S(2)}, u32[]{:S(2)}) collective-permute-start(bf16[1536,384]{1,0:T(8,128)(2,1)} %reshape.210), channel_id=1, source_target_pairs={{0,2},{1,3},{2,0},{3,1},{4,6},{5,7},{6,4},{7,5},{8,10},{9,11},{10,... | collective-permute-start | bytes 3538952 | tf_op jit(solution)/shard_map/ppermute | solution.py:111
  190.1 50.4 %collective-permute-start.3 = (bf16[1536,384]{1,0:T(8,128)(2,1)}, bf16[1536,384]{1,0:T(8,128)(2,1)}, u32[]{:S(2)}, u32[]{:S(2)}) collective-permute-start(bf16[1536,384]{1,0:T(8,128)(2,1)} %reshape.210), channel_id=1, source_target_pairs={{0,3},{1,0},{2,1},{3,2},{4,7},{5,4},{6,5},{7,6},{8,11},{9,8},{10,9... | collective-permute-start | bytes 3538952 | tf_op jit(solution)/shard_map/ppermute | solution.py:111
  249.7 30.9 %collective-permute-start.4 = (bf16[1536,384]{1,0:T(8,128)(2,1)}, bf16[1536,384]{1,0:T(8,128)(2,1)S(1)}, u32[]{:S(2)}, u32[]{:S(2)}) collective-permute-start(bf16[1536,384]{1,0:T(8,128)(2,1)} %convolution_convert_fusion.2), channel_id=1, source_target_pairs={{0,1},{1,2},{2,3},{3,0},{4,5},{5,6},{6,7},{7,4},{8,9},{9,10},{10,1... | collective-permute-start | bytes 3538952 | tf_op jit(solution)/shard_map/ppermute | solution.py:135
  254.5 52.6 %collective-permute-start.5 = (bf16[1536,384]{1,0:T(8,128)(2,1)}, bf16[1536,384]{1,0:T(8,128)(2,1)}, u32[]{:S(2)}, u32[]{:S(2)}) collective-permute-start(bf16[1536,384]{1,0:T(8,128)(2,1)} %convolution_convert_fusion.1), channel_id=1, source_target_pairs={{0,2},{1,3},{2,0},{3,1},{4,6},{5,7},{6,4},{7,5},{8,10},{9,11},{10,... | collective-permute-start | bytes 3538952 | tf_op jit(solution)/shard_map/ppermute | solution.py:135
  261.4 49.0 %collective-permute-start.6 = (bf16[1536,384]{1,0:T(8,128)(2,1)}, bf16[1536,384]{1,0:T(8,128)(2,1)}, u32[]{:S(2)}, u32[]{:S(2)}) collective-permute-start(bf16[1536,384]{1,0:T(8,128)(2,1)} %convolution_convert_fusion), channel_id=1, source_target_pairs={{0,3},{1,0},{2,1},{3,2},{4,7},{5,4},{6,5},{7,6},{8,11},{9,8},{10,9... | collective-permute-start | bytes 3538952 | tf_op jit(solution)/shard_map/ppermute | solution.py:135
  280.6 26.6 %copy-start.3 = (bf16[1536,384]{1,0:T(8,128)(2,1)}, bf16[1536,384]{1,0:T(8,128)(2,1)S(1)}, u32[]{:S(2)}) copy-start(bf16[1536,384]{1,0:T(8,128)(2,1)S(1)} %collective-permute-done.4) | copy-start | bytes 3538948
  314.8 9.1 %copy-start.8 = (f32[128,4]{0,1:T(4,128)S(1)}, f32[128,4]{0,1:T(4,128)}, u32[]{:S(2)}) copy-start(f32[128,4]{0,1:T(4,128)} %param.21) | copy-start | bytes 6148
  314.8 51.1 %all-to-all-start.2 = ((bf16[128,12,384]{2,1,0:T(8,128)(2,1)}), bf16[128,12,384]{2,1,0:T(8,128)(2,1)}, u32[]{:S(2)}, u32[]{:S(2)}) async-start(bf16[128,12,384]{2,1,0:T(8,128)(2,1)} %reshape.213), calls=%async_computation.2 | async-start | bytes 3145728 | tf_op jit(solution)/shard_map/all_to_all | solution.py:139
  370.1 0.9 copy-start.2
  370.1 0.9 copy-start.5
Sparse Core Ops, SparseCore 0:
  83.4 21.9 reduce-scatter.3
